TPU v7x, 128 devices: a whole 4x4x4 slice. The times are simulated.
128 devices in a mesh: req: 16 (over y, z), mp: 8 (over x, core).
Axes of the slice: x: 4, y: 4, z: 4, core: 2. Of those that a mesh axis runs over, the one named last changes fastest.
Arguments:
- hidden_in: bfloat16 [16384, 2048], P('req', 'mp'), may hold values from -6 to 6
- w_qkv: bfloat16 [3, 2048, 2048], P(None, 'req', 'mp'), may hold values from -0.125 to 0.125
- w_out: bfloat16 [2048, 2048], P('mp', 'req'), may hold values from -0.125 to 0.125
- attn_gain: bfloat16 [2048], replicated, may hold values from 0.099609375 to 1.8984375
- mlp_gain: bfloat16 [2048], replicated, may hold values from 0.099609375 to 1.8984375
- w_gate: bfloat16 [2048, 8192], P('req', 'mp'), may hold values from -0.125 to 0.125
- w_up: bfloat16 [2048, 8192], P('req', 'mp'), may hold values from -0.125 to 0.125
- w_down: bfloat16 [8192, 2048], P('mp', 'req'), may hold values from -0.0625 to 0.0625
- k_cache: bfloat16 [16, 4096, 2048], P('req', None, 'mp'), may hold values from -363 to 363
- v_cache: bfloat16 [16, 4096, 2048], P('req', None, 'mp'), may hold values from -6 to 6
- cache_len: int32 [16], P('req'), may hold values from 256 to 4096, as said below
Outputs:
- hidden_out: bfloat16 [16384, 2048], P('req', 'mp')
- new_keys: bfloat16 [16384, 2048], P('req', 'mp')
- new_values: bfloat16 [16384, 2048], P('req', 'mp')
Inputs may be any that keep to these rules, and one draw needn't show every extreme that they name: Each request uses its first cache_len slots; later slots hold unused data. Some request's cache is full in every draw.
All inputs are finite; a program needn't handle non-finite values.
Results may differ from a plain program's by a relative error of at most 0.02.
Values may be sent and summed in bfloat16 or wider, within the bound.
No kernel may reach another device: no remote copies, remote signals or barrier semaphores. Data moves between devices by JAX's collectives and lax.ppermute only.
A program may use at most 128 MiB of HBM per device.

v0:
```python
import jax
import jax.numpy as jnp
from jax import lax
from jax.sharding import PartitionSpec as P

HD = 64
THETA = 130000.0
EPSILON = 1e-05
NEG_FILL = -1e30


def rms_scale(rows, gain):
    values = rows.astype(jnp.float32)
    meansq = jnp.mean(values * values, axis=-1, keepdims=True)
    return (values * lax.rsqrt(meansq + EPSILON) * gain.astype(jnp.float32)).astype(jnp.bfloat16)


def rotate(tensor, positions):
    half = tensor.shape[-1] // 2
    freq = THETA ** (-(jnp.arange(half, dtype=jnp.float32) * 2.0 / tensor.shape[-1]))
    angle = positions[:, None, None] * freq[None, None, :]
    cosine = jnp.cos(angle)
    sine = jnp.sin(angle)
    first = tensor[..., :half]
    second = tensor[..., half:]
    return jnp.concatenate(
        [first * cosine - second * sine, second * cosine + first * sine], axis=-1
    )


def gather_packed(blocks, axes, axis_name):
    count = lax.axis_size(axis_name)
    lane = 128
    joined = jnp.concatenate([block.reshape(-1, lane) for block in blocks], axis=0)
    gathered = lax.all_gather(joined, axis_name, axis=0, tiled=False)
    outs = []
    offset = 0
    for block, axis in zip(blocks, axes):
        rows = block.size // lane
        piece = gathered[:, offset : offset + rows].reshape((count,) + block.shape)
        piece = jnp.moveaxis(piece, 0, axis)
        shape = list(block.shape)
        shape[axis] *= count
        outs.append(piece.reshape(shape))
        offset += rows
    return outs


def absorb(carry, queries, keys, values, valid):
    top, total, accum = carry
    scores = jnp.einsum("qhd,khd->hqk", queries, keys, preferred_element_type=jnp.float32) * HD ** (
        -0.5
    )
    scores = jnp.where(valid[None], scores, NEG_FILL)
    new_top = jnp.maximum(top, jnp.max(scores, axis=-1, keepdims=True))
    factor = jnp.exp(top - new_top)
    probs = jnp.where(valid[None], jnp.exp(scores - new_top), 0.0)
    total = total * factor + jnp.sum(probs, axis=-1, keepdims=True)
    accum = accum * factor + jnp.einsum(
        "hqk,khd->hqd", probs.astype(jnp.bfloat16), values, preferred_element_type=jnp.float32
    )
    return (new_top, total, accum)


def on_device(
    hidden_in, w_qkv, w_out, attn_gain, mlp_gain, w_gate, w_up, w_down, k_cache, v_cache, cache_len
):
    new_count = hidden_in.shape[0]
    w_qkv_full = lax.all_gather(w_qkv, "req", axis=1, tiled=True)
    w_gate_full, w_up_full, w_down_full, w_out_full = gather_packed(
        [w_gate, w_up, w_down, w_out], [0, 0, 1, 1], "req"
    )
    width = w_qkv.shape[2]
    heads_local = width // HD
    slots = k_cache.shape[1]
    full_rows = lax.all_gather(hidden_in, "mp", axis=1, tiled=True)
    normed = rms_scale(full_rows, attn_gain)
    columns = normed
    projected = jnp.einsum("nd,kdw->knw", columns, w_qkv_full, preferred_element_type=jnp.float32)
    length = cache_len[0]
    positions = (length + jnp.arange(new_count, dtype=jnp.int32)).astype(jnp.float32)
    queries = rotate(projected[0].reshape(new_count, heads_local, HD), positions).astype(
        jnp.bfloat16
    )
    fresh_keys = rotate(projected[1].reshape(new_count, heads_local, HD), positions).astype(
        jnp.bfloat16
    )
    fresh_values = projected[2].astype(jnp.bfloat16).reshape(new_count, heads_local, HD)
    rows = jnp.arange(new_count, dtype=jnp.int32)
    causal = rows[:, None] >= rows[None, :]
    start_carry = (
        jnp.full((heads_local, new_count, 1), NEG_FILL, jnp.float32),
        jnp.zeros((heads_local, new_count, 1), jnp.float32),
        jnp.zeros((heads_local, new_count, HD), jnp.float32),
    )
    carry = absorb(start_carry, queries, fresh_keys, fresh_values, causal)
    cache_keys = k_cache[0].reshape(slots, heads_local, HD)
    cache_values = v_cache[0].reshape(slots, heads_local, HD)
    block = min(slots, 512)
    count = (length + block - 1) // block

    def step_block(index, state):
        begin = index * block
        keys = lax.dynamic_slice_in_dim(cache_keys, begin, block, 0)
        values = lax.dynamic_slice_in_dim(cache_values, begin, block, 0)
        valid = (begin + jnp.arange(block, dtype=jnp.int32) < length)[None, :]
        return absorb(state, queries, keys, values, valid)

    top, total, accum = lax.fori_loop(0, count, step_block, carry)
    attn = (accum / total).transpose(1, 0, 2).reshape(new_count, width).astype(jnp.bfloat16)
    partial_value = jnp.dot(attn, w_out_full, preferred_element_type=jnp.float32)
    summed = lax.psum(partial_value.astype(jnp.bfloat16), "mp").astype(jnp.float32)
    mid_full = (full_rows.astype(jnp.float32) + summed).astype(jnp.bfloat16)
    own = hidden_in.shape[1]
    mid_local = lax.dynamic_slice_in_dim(mid_full, lax.axis_index("mp") * own, own, axis=1)
    normed2 = rms_scale(mid_full, mlp_gain)
    columns = normed2
    gate = jnp.dot(columns, w_gate_full, preferred_element_type=jnp.float32)
    upper = jnp.dot(columns, w_up_full, preferred_element_type=jnp.float32)
    units = (jax.nn.silu(gate) * upper).astype(jnp.bfloat16)
    terms = jnp.dot(units, w_down_full, preferred_element_type=jnp.float32)
    reduced = lax.psum_scatter(
        terms.astype(jnp.bfloat16), "mp", scatter_dimension=1, tiled=True
    ).astype(jnp.float32)
    hidden_out = (mid_local.astype(jnp.float32) + reduced).astype(jnp.bfloat16)
    return (
        hidden_out,
        fresh_keys.reshape(new_count, width),
        fresh_values.reshape(new_count, width),
    )


def solution(mesh):
    return jax.shard_map(
        on_device,
        mesh=mesh,
        in_specs=(
            P("req", "mp"),
            P(None, "req", "mp"),
            P("mp", "req"),
            P(),
            P(),
            P("req", "mp"),
            P("req", "mp"),
            P("mp", "req"),
            P("req", None, "mp"),
            P("req", None, "mp"),
            P("req"),
        ),
        out_specs=(P("req", "mp"), P("req", "mp"), P("req", "mp")),
        check_vma=False,
    )
```

profile of v0, /device:TPU:0, one launch (start us, length us, event | category | flops | bytes accessed | tf_op | source)
XLA Modules:
  0.0 353.1 jit_solution(15132475671423839923)
XLA Ops:
  7.2 0.7 all-gather.5.cloned.1.call-update
  8.0 1.7 copy.29
  9.7 0.0 all-gather.9.cloned.1.call-start
  9.8 1.1 reshape.167
  10.8 1.1 reshape.168
  11.9 2.0 pad_maximum_fusion
  14.6 2.9 copy.31
  17.6 4.1 %copy.32 = bf16[1,4096,256]{1,2,0:T(8,128)(2,1)} copy(bf16[1,4096,256]{2,1,0:T(8,128)(2,1)} %param.22) | data formatting | bytes 4194304 | tf_op args[9]
  21.7 1.3 iota_compare_fusion
  23.0 0.5 multiply_cosine_fusion
  23.5 24.7 %all-gather.5.cloned.1.call-done = bf16[1024,2048]{1,0:T(8,128)(2,1)} async-done(((bf16[1024,256]{1,0:T(8,128)(2,1)}), bf16[1024,2048]{1,0:T(8,128)(2,1)}) %all-gather.5.cloned.1.call-update) | async-done | bytes 4194320 | tf_op jit(solution)/shard_map/all_gather | solution.py:76
  48.2 3.1 fusion.26
  51.3 53.4 %all-gather.7.cloned.1.call-done = bf16[3,2048,256]{1,2,0:T(8,128)(2,1)} async-done(((bf16[3,128,256]{1,2,0:T(8,128)(2,1)}), bf16[3,2048,256]{1,2,0:T(8,128)(2,1)}) %all-gather.7.cloned.1.call-update) | async-done | bytes 3145744 | tf_op jit(solution)/shard_map/all_gather | solution.py:69
  104.7 6.6 %fusion.38 = f32[3,1024,256]{1,2,0:T(8,128)S(1)} fusion(bf16[3,2048,256]{1,2,0:T(8,128)(2,1)} %all-gather.7.cloned.1.call-done, bf16[1024,2048]{1,0:T(8,128)(2,1)} %all-gather.5.cloned.1.call-done, f32[2048]{0:T(1024)S(1)} %convert_element_type.84, f32[1024]{0:T(1024)S(1)} %add_rsqrt_fusion.1), kind=kOutput, calls=%fused_computation.52 | convolution fusion | flops 3229614080 | bytes 10498048 | tf_op jit(solution)/shard_map/nd,kdw->knw/dot_general | solution.py:79
  111.3 1.0 slice.66
  112.3 0.1 fusion.57
  112.4 0.2 subtract_convert_fusion
  112.6 0.2 multiply_subtract_fusion
  112.8 0.3 copy-done.3
  113.1 0.7 copy-done.1
  113.8 3.0 fusion.20
  116.8 4.2 %fusion.22 = f32[4,1024]{1,0:T(4,128)S(1)} fusion(f32[4,1024,1024]{1,2,0:T(8,128)S(1)} %get-tuple-element.102, f32[4,1024]{1,0:T(4,128)S(1)} %get-tuple-element.98, pred[1024,1024]{0,1:T(8,128)(4,1)S(1)} %copy-done.1), kind=kLoop, calls=%fused_computation.31 | loop fusion | flops 20967424 | bytes 17858560 | tf_op jit(solution)/shard_map/reduce_sum | solution.py:58
  121.1 5.9 %fusion.41 = f32[4,1024,64]{1,2,0:T(8,128)} fusion(bf16[1024,4,64]{0,2,1:T(8,128)(2,1)S(1)} %bitcast.91, f32[4,1024,1024]{1,2,0:T(8,128)S(1)} %get-tuple-element.102, f32[4,1024]{1,0:T(4,128)S(1)} %get-tuple-element.98, pred[1024,1024]{0,1:T(8,128)(4,1)S(1)} %copy-done.1, f32[4,1024]{1,0:T(4,128)S(1)} %get-tuple-element.96), kind=kOutput, calls=%fused_computation.53 | convolution fusion | flops 558104576 | bytes 19431424 | tf_op jit(solution)/shard_map/hqk,khd->hqd/dot_general | solution.py:59
  127.0 8.0 %while.14 = (s32[]{:T(128)}, f32[4,1024,1]{1,0,2:T(4,128)S(1)}, f32[4,1024,1]{1,0,2:T(4,128)S(1)}, f32[4,1024,64]{1,2,0:T(8,128)}, s32[]{:T(128)}, /*index=5*/s3...) while((s32[]{:T(128)}, f32[4,1024,1]{1,0,2:T(4,128)S(1)}, ...), condition=%wide.region_6.7_spmd, body=%wide.region_3.6_spmd.sunk | while | flops 564671488 | bytes 36965104 | solution.py:109
  127.0 0.7 add_compare_fusion.2
  127.7 1.6 bitcast_reduce_fusion.2
  129.3 3.1 fusion.77
  132.4 2.5 fusion.76
  135.0 1.3 divide_convert_fusion
  136.3 65.2 %all-gather.9.cloned.1.call-done = bf16[53248,128]{1,0:T(8,128)(2,1)} async-done(((bf16[3328,128]{1,0:T(8,128)(2,1)}), bf16[53248,128]{1,0:T(8,128)(2,1)}) %all-gather.9.cloned.1.call-update) | async-done | bytes 13631504 | tf_op jit(solution)/shard_map/all_gather | solution.py:35
  201.5 1.3 slice_bitcast_fusion.1
  202.8 0.5 copy.33
  203.4 3.3 convolution_convert_fusion
  206.7 0.3 reduce-scatter.2.cloned.1.call-start
  207.0 0.4 copy-done.8
  207.4 9.1 %fusion.56 = (bf16[16,1024,128]{2,1,0:T(8,128)(2,1)}, bf16[1024,16,128]{2,0,1:T(8,128)(2,1)}, bf16[16,1024,128]{2,1,0:T(8,128)(2,1)}) fusion(bf16[16,3328,128]{2,1,0:T(8,128)(2,1)} %bitcast.79), kind=kLoop, calls=%fused_computation.81 | loop fusion | bytes 25165824 | tf_op jit(solution)/shard_map/slice | solution.py:40
  216.5 7.4 %reshape_reshape.6 = bf16[2048,1024]{1,0:T(8,128)(2,1)} reshape(bf16[16,1024,128]{2,1,0:T(8,128)(2,1)} %get-tuple-element.89) | data formatting | bytes 8388608 | tf_op jit(solution)/shard_map/reshape;reshape | solution.py:44
  223.9 6.4 %copy.34 = bf16[1024,16,128]{0,2,1:T(8,128)(2,1)} copy(bf16[1024,16,128]{2,0,1:T(8,128)(2,1)} %get-tuple-element.88) | data formatting | bytes 8388608 | tf_op jit(solution)/shard_map/transpose | solution.py:41
  230.4 7.4 %reshape_reshape.7 = bf16[2048,1024]{1,0:T(8,128)(2,1)} reshape(bf16[16,1024,128]{2,1,0:T(8,128)(2,1)} %get-tuple-element.87) | data formatting | bytes 8388608 | tf_op jit(solution)/shard_map/reshape;reshape | solution.py:44
  237.8 41.3 %all-reduce.2.cloned.1.call-done = bf16[1024,2048]{1,0:T(8,128)(2,1)} async-done(((bf16[1024,2048]{1,0:T(8,128)(2,1)}), bf16[1024,2048]{1,0:T(8,128)(2,1)}) %all-reduce.2.cloned.1.call-update) | async-done | bytes 4194320 | tf_op jit(solution)/shard_map/psum | solution.py:112
  279.0 5.6 %fusion.23 = (f32[1024]{0:T(1024)S(1)}, bf16[1024,2048]{1,0:T(8,128)(2,1)S(1)}) fusion(bf16[1024,2048]{1,0:T(8,128)(2,1)} %all-reduce.2.cloned.1.call-done, bf16[1024,2048]{1,0:T(8,128)(2,1)} %all-gather.5.cloned.1.call-done), kind=kLoop, calls=%fused_computation.34 | loop fusion | flops 14679040 | bytes 12587008 | tf_op jit(solution)/shard_map/reduce_sum | solution.py:14
  284.7 6.3 %fusion.45 = f32[1024,1024]{1,0:T(8,128)} fusion(bf16[2048,1024]{1,0:T(8,128)(2,1)S(1)} %copy-done.2, bf16[1024,2048]{1,0:T(8,128)(2,1)S(1)} %get-tuple-element.84, f32[2048]{0:T(1024)S(1)} %convert_element_type.99, f32[1024]{0:T(1024)S(1)} %add_rsqrt_fusion), kind=kOutput, calls=%fused_computation.54 | convolution fusion | flops 4303355904 | bytes 12595200 | tf_op jit(solution)/shard_map/dot_general | solution.py:118
  291.0 15.4 %convolution_convert_fusion.1 = bf16[1024,2048]{1,0:T(8,128)(2,1)} fusion(bf16[1024,2048]{0,1:T(8,128)(2,1)} %bitcast.84, f32[1024,1024]{1,0:T(8,128)} %fusion.45, bf16[2048,1024]{1,0:T(8,128)(2,1)} %reshape_reshape.7, bf16[1024,2048]{1,0:T(8,128)(2,1)} %copy-done, f32[2048]{0:T(1024)S(1)} %convert_element_type.99, f32[1024]{0:T(1024)S(1)} %add_rsqrt_fusion), kind=kOutput, calls=%fused_computation.51 | convolution fusion | flops 8606711808 | bytes 20983808 | tf_op jit(solution)/shard_map/dot_general | solution.py:121
  306.4 1.0 copy.35
  307.4 1.3 slice_bitcast_fusion.2
  308.7 1.0 copy.36
  309.7 34.8 %reduce-scatter.2.cloned.1.call-done = bf16[1024,256]{1,0:T(8,128)(2,1)} async-done(((bf16[1024,2048]{1,0:T(8,128)(2,1)}), bf16[1024,256]{1,0:T(8,128)(2,1)}) %reduce-scatter.2.cloned.1.call-update) | async-done | bytes 524304 | tf_op jit(solution)/shard_map/reduce_scatter | solution.py:122
  344.5 2.1 add_convert_fusion
  (35 shorter events, 0.4 us)
Async XLA Ops:
  7.2 7.4 %copy-start.7 = (bf16[2048]{0:T(1024)(128)(2,1)S(1)}, bf16[2048]{0:T(1024)(128)(2,1)}, u32[]{:S(2)}) copy-start(bf16[2048]{0:T(1024)(128)(2,1)} %param.16) | copy-start | bytes 12292
  7.2 41.0 %all-gather.5.cloned.1.call-start = ((), (), s32[]{:S(2)}) async-start(), calls=%async_computation.1 | async-start | bytes 4718592 | tf_op jit(solution)/shard_map/all_gather | solution.py:76
  7.9 96.8 %all-gather.7.cloned.1.call-start = ((), (), s32[]{:S(2)}) async-start(), calls=%async_computation.2 | async-start | bytes 3342336 | tf_op jit(solution)/shard_map/all_gather | solution.py:69
  9.7 191.8 %all-gather.9.cloned.1.call-start = ((), (), s32[]{:S(2)}) async-start(), calls=%async_computation.5 | async-start | bytes 14483456 | tf_op jit(solution)/shard_map/all_gather | solution.py:35
  13.9 265.1 %all-reduce.2.cloned.1.call-start = ((), (), s32[]{:S(2)}) async-start(), calls=%async_computation.3 | async-start | bytes 8388608 | tf_op jit(solution)/shard_map/psum | solution.py:112
  111.3 1.8 copy-start.3
  112.3 1.5 copy-start.1
  116.8 4.2 %copy-start.6 = (bf16[1,1024,256]{1,2,0:T(8,128)(2,1)S(1)}, bf16[1,1024,256]{1,2,0:T(8,128)(2,1)}, u32[]{:S(2)}) copy-start(bf16[1,1024,256]{1,2,0:T(8,128)(2,1)} %slice.66) | copy-start | bytes 1572868
  127.7 1.6 copy-start.4
  132.4 2.6 copy-start.5
  206.7 0.7 copy-start.8
  206.7 137.7 %reduce-scatter.2.cloned.1.call-start = ((), (), s32[]{:S(2)}) async-start(), calls=%async_computation.4 | async-start | bytes 4718592 | tf_op jit(solution)/shard_map/reduce_scatter | solution.py:122
  279.0 5.6 %copy-start.2 = (bf16[2048,1024]{1,0:T(8,128)(2,1)S(1)}, bf16[2048,1024]{1,0:T(8,128)(2,1)}, u32[]{:S(2)}) copy-start(bf16[2048,1024]{1,0:T(8,128)(2,1)} %reshape_reshape.6) | copy-start | bytes 12582916
  284.6 6.4 %copy-start = (bf16[1024,2048]{1,0:T(8,128)(2,1)}, bf16[1024,2048]{1,0:T(8,128)(2,1)S(1)}, u32[]{:S(2)}) copy-start(bf16[1024,2048]{1,0:T(8,128)(2,1)S(1)} %get-tuple-element.84) | copy-start | bytes 12582916
Sparse Core Ops, SparseCore 0:
  9.7 38.4 all-gather.4
  50.9 53.7 all-gather.6
  106.9 94.6 all-gather.8
  206.9 72.1 all-reduce.1
  306.5 37.9 reduce-scatter.1
where the time goes:
time: 354 us; the launch traced here: 353 us
  waiting for transfers between devices  220 us (62%)
  local copies, waits for them, and re-layouts  48.9 us (14%)
  matrix products  45.3 us (13%)
  other arithmetic  23.8 us (7%)
  between operations  14.7 us (4%)
    all_gather x1, waiting for transfers between devices, gather_packed(): gathered = lax.all_gather(joined, axis_name, axis=0, tiled=False)  65.2 us
    all_gather x1, waiting for transfers between devices, on_device(): w_qkv_full = lax.all_gather(w_qkv, 'req', axis=1, tiled=True)  53.4 us
    psum x1, waiting for transfers between devices, on_device(): lax.psum(partial_value.astype(jnp.bfloat16), 'mp').astype(jnp.float32)  41.3 us
    reduce_scatter x1, waiting for transfers between devices, on_device(): lax.psum_scatter(terms.astype(jnp.bfloat16), 'mp', scatter_dimension=1, t...  34.8 us
    all_gather x1, waiting for transfers between devices, on_device(): full_rows = lax.all_gather(hidden_in, 'mp', axis=1, tiled=True)  24.7 us
    dot_general x1, matrix products, on_device(): terms = jnp.dot(units, w_down_full, preferred_element_type=jnp.float32)  15.4 us
    another operation x2, local copies, waits for them, and re-layouts, gather_packed(): outs.append(piece.reshape(shape))  14.8 us
    unnamed x19, local copies, waits for them, and re-layouts  12.2 us
  transfers between devices with their start and end apart: 5, of which 5 were waited for; matrix products, arithmetic and copies ran while one was open for 23% of the time, Pallas kernels for 0%

commit v1 on v0

--- a/solution.py
+++ b/solution.py
@@ -7,6 +7,11 @@
 THETA = 130000.0
 EPSILON = 1e-05
 NEG_FILL = -1e30
+
+
+def swapped_in(x, name, dim):
+    stack = jnp.stack([x] * lax.axis_size(name))
+    return jnp.concatenate(lax.all_to_all(stack, name, 0, 0), axis=dim)
 
 
 def rms_scale(rows, gain):
@@ -73,7 +78,7 @@
     width = w_qkv.shape[2]
     heads_local = width // HD
     slots = k_cache.shape[1]
-    full_rows = lax.all_gather(hidden_in, "mp", axis=1, tiled=True)
+    full_rows = swapped_in(hidden_in, "mp", 1)
     normed = rms_scale(full_rows, attn_gain)
     columns = normed
     projected = jnp.einsum("nd,kdw->knw", columns, w_qkv_full, preferred_element_type=jnp.float32)

time: 354 us -> 322 us (0.910)
  waiting for transfers between devices: 220 us -> 172 us
  local copies, waits for them, and re-layouts: 48.9 us -> 55.6 us
  starting transfers between devices: 0.42 us -> 4.88 us
  other arithmetic: 23.8 us -> 27.5 us
    all_gather x1, waiting for transfers between devices: 53.4 us -> 0.02 us  [on_device(): w_qkv_full = lax.all_gather(w_qkv, 'req', axis=1, tiled=True)]
    all_to_all x0 -> x1, waiting for transfers between devices: none -> 40 us  [swapped_in(): return jnp.concatenate(lax.all_to_all(stack, name, 0, 0), axis=dim)]
    all_gather x1 -> x0, waiting for transfers between devices: 24.7 us -> none  [on_device(): full_rows = lax.all_gather(hidden_in, 'mp', axis=1, tiled=True)]
    all_gather x1, waiting for transfers between devices: 65.2 us -> 49.7 us  [gather_packed(): gathered = lax.all_gather(joined, axis_name, axis=0, tiled=False)]
    psum x1, waiting for transfers between devices: 41.3 us -> 47.2 us  [on_device(): lax.psum(partial_value.astype(jnp.bfloat16), 'mp').astype(jnp.float32)]
    all_to_all x0 -> x1, starting transfers between devices: none -> 4.71 us  [swapped_in(): return jnp.concatenate(lax.all_to_all(stack, name, 0, 0), axis=dim)]
    convert_element_type x0 -> x1, local copies, waits for them, and re-layouts: none -> 4.28 us  [on_device(): mid_full = (full_rows.astype(jnp.float32) + summed).astype(jnp.bfloat16)]
    unnamed x19 -> x21, local copies, waits for them, and re-layouts: 12.2 us -> 12.4 us
  transfers between devices with their start and end apart: 5 -> 5, of which waited for: 5 -> 4; matrix products, arithmetic and copies ran while one was open for 23% -> 28% of each run, Pallas kernels for 0% -> 0%
where the time goes in v1:
time: 322 us; the launch traced here: 321 us
  waiting for transfers between devices  172 us (53%)
  local copies, waits for them, and re-layouts  55.6 us (17%)
  matrix products  46.1 us (14%)
  other arithmetic  27.5 us (9%)
  between operations  14.7 us (5%)
  starting transfers between devices  4.88 us (2%)
    all_gather x1, waiting for transfers between devices, gather_packed(): gathered = lax.all_gather(joined, axis_name, axis=0, tiled=False)  49.7 us
    psum x1, waiting for transfers between devices, on_device(): lax.psum(partial_value.astype(jnp.bfloat16), 'mp').astype(jnp.float32)  47.2 us
    all_to_all x1, waiting for transfers between devices, swapped_in(): return jnp.concatenate(lax.all_to_all(stack, name, 0, 0), axis=dim)  40 us
    reduce_scatter x1, waiting for transfers between devices, on_device(): lax.psum_scatter(terms.astype(jnp.bfloat16), 'mp', scatter_dimension=1, t...  34.8 us
    dot_general x1, matrix products, on_device(): terms = jnp.dot(units, w_down_full, preferred_element_type=jnp.float32)  15.4 us
    another operation x2, local copies, waits for them, and re-layouts, gather_packed(): outs.append(piece.reshape(shape))  14.8 us
    unnamed x21, local copies, waits for them, and re-layouts  12.4 us
    reduce_sum x2, other arithmetic, rms_scale(): meansq = jnp.mean(values * values, axis=-1, keepdims=True)  9.45 us
  transfers between devices with their start and end apart: 5, of which 4 were waited for; matrix products, arithmetic and copies ran while one was open for 28% of the time, Pallas kernels for 0%

profile of v1, /device:TPU:0, one launch (start us, length us, event | category | flops | bytes accessed | tf_op | source)
XLA Modules:
  0.0 320.7 jit_solution(11449471889414298141)
XLA Ops:
  7.2 1.8 copy.39
  9.1 1.1 reshape.173
  10.2 1.1 reshape.174
  11.2 2.0 pad_maximum_fusion
  13.2 2.2 stack.2
  15.4 4.7 %all-to-all-start = ((bf16[8,1024,256]{2,1,0:T(8,128)(2,1)}), bf16[8,1024,256]{2,1,0:T(8,128)(2,1)}, u32[]{:S(2)}, u32[]{:S(2)}) async-start(bf16[8,1024,256]{2,1,0:T(8,128)(2,1)} %stack.2), calls=%async_computation | async-start | bytes 8388608 | tf_op jit(solution)/shard_map/all_to_all | solution.py:14
  20.9 2.9 copy.41
  23.9 4.1 %copy.42 = bf16[1,4096,256]{1,2,0:T(8,128)(2,1)} copy(bf16[1,4096,256]{2,1,0:T(8,128)(2,1)} %param.22) | data formatting | bytes 4194304 | tf_op args[9]
  28.0 1.3 iota_compare_fusion
  29.3 0.5 multiply_cosine_fusion
  29.8 40.0 %all-to-all-done = bf16[8,1024,256]{2,1,0:T(8,128)(2,1)} async-done(((bf16[8,1024,256]{2,1,0:T(8,128)(2,1)}), bf16[8,1024,256]{2,1,0:T(8,128)(2,1)}, u32[]{:S(2)}, u32[]{:S(2)}) %all-to-all-start) | async-done | bytes 4194336 | tf_op jit(solution)/shard_map/all_to_all | solution.py:14
  69.8 2.9 convert_bitcast_fusion
  72.8 4.3 %copy.49 = f32[8,128,8,256]{3,2,0,1:T(8,128)} copy(f32[8,128,8,256]{3,2,1,0:T(8,128)S(1)} %convert_bitcast_fusion) | data formatting | bytes 16777216 | tf_op jit(solution)/shard_map/convert_element_type | solution.py:118
  77.1 3.4 %fusion.26 = f32[1024]{0:T(1024)S(1)} fusion(bf16[8,1024,256]{2,1,0:T(8,128)(2,1)} %all-to-all-done), kind=kLoop, calls=%fused_computation.36 | loop fusion | flops 6290432 | bytes 4198400 | tf_op jit(solution)/shard_map/reduce_sum | solution.py:19
  80.5 7.3 %fusion.35 = f32[3,1024,256]{1,2,0:T(8,128)S(1)} fusion(bf16[3,2048,256]{1,2,0:T(8,128)(2,1)} %all-gather.4.cloned.1.call-done, f32[1024,2048]{1,0:T(8,128)} %bitcast.82, f32[2048]{0:T(1024)S(1)} %convert_element_type.97, f32[1024]{0:T(1024)S(1)} %add_rsqrt_fusion.1), kind=kOutput, calls=%fused_computation.50 | convolution fusion | flops 3227516928 | bytes 14692352 | tf_op jit(solution)/shard_map/nd,kdw->knw/dot_general | solution.py:84
  87.8 1.0 slice.66
  88.9 0.2 fusion.53
  89.1 0.2 subtract_convert_fusion
  89.3 0.2 multiply_subtract_fusion
  89.5 0.2 copy-done.3
  89.6 0.7 copy-done.1
  90.3 3.0 fusion.20
  93.4 4.2 %fusion.22 = f32[4,1024]{1,0:T(4,128)S(1)} fusion(f32[4,1024,1024]{1,2,0:T(8,128)S(1)} %get-tuple-element.105, f32[4,1024]{1,0:T(4,128)S(1)} %get-tuple-element.101, pred[1024,1024]{0,1:T(8,128)(4,1)S(1)} %copy-done.1), kind=kLoop, calls=%fused_computation.28 | loop fusion | flops 20967424 | bytes 17858560 | tf_op jit(solution)/shard_map/reduce_sum | solution.py:63
  97.6 6.2 %fusion.38 = f32[4,1024,64]{1,2,0:T(8,128)} fusion(bf16[1024,4,64]{0,2,1:T(8,128)(2,1)S(1)} %bitcast.97, f32[4,1024,1024]{1,2,0:T(8,128)S(1)} %get-tuple-element.105, f32[4,1024]{1,0:T(4,128)S(1)} %get-tuple-element.101, pred[1024,1024]{0,1:T(8,128)(4,1)S(1)} %copy-done.1, f32[4,1024]{1,0:T(4,128)S(1)} %get-tuple-element.99), kind=kOutput, calls=%fused_computation.51 | convolution fusion | flops 558104576 | bytes 19431424 | tf_op jit(solution)/shard_map/hqk,khd->hqd/dot_general | solution.py:64
  103.8 8.0 %while.14 = (s32[]{:T(128)}, f32[4,1024,1]{1,0,2:T(4,128)S(1)}, f32[4,1024,1]{1,0,2:T(4,128)S(1)}, f32[4,1024,64]{1,2,0:T(8,128)}, s32[]{:T(128)}, /*index=5*/s3...) while((s32[]{:T(128)}, f32[4,1024,1]{1,0,2:T(4,128)S(1)}, ...), condition=%wide.region_6.7_spmd, body=%wide.region_3.6_spmd.sunk | while | flops 564671488 | bytes 36965104 | solution.py:114
  103.8 0.7 add_compare_fusion.2
  104.5 1.6 bitcast_reduce_fusion.2
  106.1 3.1 fusion.73
  109.2 2.5 fusion.72
  111.8 1.3 divide_convert_fusion
  113.1 49.7 %all-gather.6.cloned.1.call-done = bf16[53248,128]{1,0:T(8,128)(2,1)} async-done(((bf16[3328,128]{1,0:T(8,128)(2,1)}), bf16[53248,128]{1,0:T(8,128)(2,1)}) %all-gather.6.cloned.1.call-update) | async-done | bytes 13631504 | tf_op jit(solution)/shard_map/all_gather | solution.py:40
  162.8 1.3 slice_bitcast_fusion.1
  164.1 0.5 copy.43
  164.6 3.4 %convolution_convert_fusion = bf16[1024,2048]{1,0:T(8,128)(2,1)} fusion(bf16[1024,256]{0,1:T(8,128)(2,1)S(1)} %bitcast.93, bf16[256,2048]{0,1:T(8,128)(2,1)S(1)} %bitcast.89), kind=kOutput, calls=%fused_computation.48 | convolution fusion | flops 1075838976 | bytes 5767168 | tf_op jit(solution)/shard_map/dot_general | solution.py:116
  168.1 0.6 copy-done.9
  168.7 9.0 %fusion.52 = (bf16[16,1024,128]{2,1,0:T(8,128)(2,1)}, bf16[1024,16,128]{2,0,1:T(8,128)(2,1)}, bf16[16,1024,128]{2,1,0:T(8,128)(2,1)}) fusion(bf16[16,3328,128]{2,1,0:T(8,128)(2,1)} %bitcast.85), kind=kLoop, calls=%fused_computation.79 | loop fusion | bytes 25165824 | tf_op jit(solution)/shard_map/slice | solution.py:45
  177.7 7.4 %reshape_reshape.6 = bf16[2048,1024]{1,0:T(8,128)(2,1)} reshape(bf16[16,1024,128]{2,1,0:T(8,128)(2,1)} %get-tuple-element.92) | data formatting | bytes 8388608 | tf_op jit(solution)/shard_map/reshape;reshape | solution.py:49
  185.2 6.4 %copy.44 = bf16[1024,16,128]{0,2,1:T(8,128)(2,1)} copy(bf16[1024,16,128]{2,0,1:T(8,128)(2,1)} %get-tuple-element.91) | data formatting | bytes 8388608 | tf_op jit(solution)/shard_map/transpose | solution.py:46
  191.6 7.4 %reshape_reshape.7 = bf16[2048,1024]{1,0:T(8,128)(2,1)} reshape(bf16[16,1024,128]{2,1,0:T(8,128)(2,1)} %get-tuple-element.90) | data formatting | bytes 8388608 | tf_op jit(solution)/shard_map/reshape;reshape | solution.py:49
  199.0 47.2 %all-reduce.2.cloned.1.call-done = bf16[1024,2048]{1,0:T(8,128)(2,1)} async-done(((bf16[1024,2048]{1,0:T(8,128)(2,1)}), bf16[1024,2048]{1,0:T(8,128)(2,1)}) %all-reduce.2.cloned.1.call-update) | async-done | bytes 4194320 | tf_op jit(solution)/shard_map/psum | solution.py:117
  246.2 6.0 %fusion.23 = (f32[1024]{0:T(1024)S(1)}, bf16[1024,2048]{1,0:T(8,128)(2,1)S(1)}) fusion(f32[1024,2048]{1,0:T(8,128)} %bitcast.83, bf16[1024,2048]{1,0:T(8,128)(2,1)} %all-reduce.2.cloned.1.call-done), kind=kLoop, calls=%fused_computation.33 | loop fusion | flops 12581888 | bytes 16781312 | tf_op jit(solution)/shard_map/reduce_sum | solution.py:19
  252.3 6.3 %fusion.42 = f32[1024,1024]{1,0:T(8,128)} fusion(bf16[2048,1024]{1,0:T(8,128)(2,1)S(1)} %copy-done.2, bf16[1024,2048]{1,0:T(8,128)(2,1)S(1)} %get-tuple-element.87, f32[2048]{0:T(1024)S(1)} %convert_element_type.112, f32[1024]{0:T(1024)S(1)} %add_rsqrt_fusion), kind=kOutput, calls=%fused_computation.52 | convolution fusion | flops 4303355904 | bytes 12595200 | tf_op jit(solution)/shard_map/dot_general | solution.py:123
  258.5 15.4 %convolution_convert_fusion.1 = bf16[1024,2048]{1,0:T(8,128)(2,1)} fusion(bf16[1024,2048]{0,1:T(8,128)(2,1)} %bitcast.90, f32[1024,1024]{1,0:T(8,128)} %fusion.42, bf16[2048,1024]{1,0:T(8,128)(2,1)} %reshape_reshape.7, bf16[1024,2048]{1,0:T(8,128)(2,1)} %copy-done, f32[2048]{0:T(1024)S(1)} %convert_element_type.112, f32[1024]{0:T(1024)S(1)} %add_rsqrt_fusion), kind=kOutput, calls=%fused_computation.49 | convolution fusion | flops 8606711808 | bytes 20983808 | tf_op jit(solution)/shard_map/dot_general | solution.py:126
  274.0 1.0 copy.45
  275.0 1.3 slice_bitcast_fusion.2
  276.3 1.0 copy.46
  277.3 34.8 %reduce-scatter.2.cloned.1.call-done = bf16[1024,256]{1,0:T(8,128)(2,1)} async-done(((bf16[1024,2048]{1,0:T(8,128)(2,1)}), bf16[1024,256]{1,0:T(8,128)(2,1)}) %reduce-scatter.2.cloned.1.call-update) | async-done | bytes 524304 | tf_op jit(solution)/shard_map/reduce_scatter | solution.py:127
  312.1 2.1 add_convert_fusion.1
  (39 shorter events, 0.5 us)
Async XLA Ops:
  7.2 6.1 %copy-start.6 = (bf16[1024,256]{1,0:T(8,128)(2,1)S(1)}, bf16[1024,256]{1,0:T(8,128)(2,1)}, u32[]{:S(2)}) copy-start(bf16[1024,256]{1,0:T(8,128)(2,1)} %param.13) | copy-start | bytes 1572868
  7.2 73.4 %all-gather.4.cloned.1.call-start = ((), (), s32[]{:S(2)}) async-start(), calls=%async_computation.2 | async-start | bytes 3342336 | tf_op jit(solution)/shard_map/all_gather | solution.py:74
  9.0 153.7 %all-gather.6.cloned.1.call-start = ((), (), s32[]{:S(2)}) async-start(), calls=%async_computation.5 | async-start | bytes 14483456 | tf_op jit(solution)/shard_map/all_gather | solution.py:40
  15.4 5.4 %copy-start.8 = (bf16[2048]{0:T(1024)(128)(2,1)S(1)}, bf16[2048]{0:T(1024)(128)(2,1)}, u32[]{:S(2)}) copy-start(bf16[2048]{0:T(1024)(128)(2,1)} %param.16) | copy-start | bytes 12292
  15.4 54.4 %all-to-all-start = ((bf16[8,1024,256]{2,1,0:T(8,128)(2,1)}), bf16[8,1024,256]{2,1,0:T(8,128)(2,1)}, u32[]{:S(2)}, u32[]{:S(2)}) async-start(bf16[8,1024,256]{2,1,0:T(8,128)(2,1)} %stack.2), calls=%async_computation | async-start | bytes 8388608 | tf_op jit(solution)/shard_map/all_to_all | solution.py:14
  20.2 226.0 %all-reduce.2.cloned.1.call-start = ((), (), s32[]{:S(2)}) async-start(), calls=%async_computation.3 | async-start | bytes 8388608 | tf_op jit(solution)/shard_map/psum | solution.py:117
  87.8 1.8 copy-start.3
  88.9 1.5 copy-start.1
  93.4 4.2 %copy-start.7 = (bf16[1,1024,256]{1,2,0:T(8,128)(2,1)S(1)}, bf16[1,1024,256]{1,2,0:T(8,128)(2,1)}, u32[]{:S(2)}) copy-start(bf16[1,1024,256]{1,2,0:T(8,128)(2,1)} %slice.66) | copy-start | bytes 1572868
  104.5 1.6 copy-start.4
  109.2 2.6 copy-start.5
  168.0 0.7 copy-start.9
  168.1 144.0 %reduce-scatter.2.cloned.1.call-start = ((), (), s32[]{:S(2)}) async-start(), calls=%async_computation.4 | async-start | bytes 4718592 | tf_op jit(solution)/shard_map/reduce_scatter | solution.py:127
  246.2 6.0 %copy-start.2 = (bf16[2048,1024]{1,0:T(8,128)(2,1)S(1)}, bf16[2048,1024]{1,0:T(8,128)(2,1)}, u32[]{:S(2)}) copy-start(bf16[2048,1024]{1,0:T(8,128)(2,1)} %reshape_reshape.6) | copy-start | bytes 12582916
  252.2 6.3 %copy-start = (bf16[1024,2048]{1,0:T(8,128)(2,1)}, bf16[1024,2048]{1,0:T(8,128)(2,1)S(1)}, u32[]{:S(2)}) copy-start(bf16[1024,2048]{1,0:T(8,128)(2,1)S(1)} %get-tuple-element.87) | copy-start | bytes 12582916
Sparse Core Ops, SparseCore 0:
  10.7 55.1 all-gather.3
  68.1 94.6 all-gather.5
  168.2 77.9 all-reduce.1
  274.0 37.9 reduce-scatter.1
